TPU v7x, 512 devices: a whole 4x4x16 slice. The times are simulated.
512 devices in a mesh: ctx: 32 (over z, core), uly: 16 (over x, y).
Axes of the slice: x: 4, y: 4, z: 16, core: 2. Of those that a mesh axis runs over, the one named last changes fastest.
Arguments:
- query_heads: bfloat16 [1, 8192, 8192], P(None, 'ctx', 'uly'), may hold values from -2.5 to 2.5
- key_heads: bfloat16 [1, 8192, 8192], P(None, 'ctx', 'uly'), may hold values from -2.5 to 2.5
- value_heads: bfloat16 [1, 8192, 8192], P(None, 'ctx', 'uly'), may hold values from -2.5 to 2.5
- grad_out: bfloat16 [1, 8192, 8192], P(None, ('ctx', 'uly')), may hold values from -2.5 to 2.5
- log_decay: float32 [1, 64, 8192], P(None, 'uly', 'ctx'), as said below
Outputs:
- attended: bfloat16 [1, 8192, 8192], P(None, ('ctx', 'uly'))
- grad_query: bfloat16 [1, 8192, 8192], P(None, ('ctx', 'uly'))
- grad_key: bfloat16 [1, 8192, 8192], P(None, ('ctx', 'uly'))
- grad_value: bfloat16 [1, 8192, 8192], P(None, ('ctx', 'uly'))
Inputs may be any that keep to these rules, and one draw needn't show every extreme that they name: `log_decay`: each entry is the logarithm of the share of a head's state that the position keeps.
All inputs are finite; a program needn't handle non-finite values.
Results may differ from a plain program's by a relative error of at most 0.0063.
Values may be sent and summed in bfloat16 or wider, within the bound.
No kernel may reach another device: no remote copies, remote signals or barrier semaphores. Data moves between devices by JAX's collectives and lax.ppermute only.
A program may use at most 64 MiB of HBM per device.

v0:
```python
import jax
import jax.numpy as jnp
from jax import lax
from jax.sharding import PartitionSpec as P


def entering(value, axis, join, neutral, backward):
    count, mine = (lax.axis_size(axis), lax.axis_index(axis))
    pieces = jax.tree.map(lambda part: lax.all_gather(part, axis), value)
    if backward:
        pieces = jax.tree.map(lambda part: part[::-1], pieces)
        mine = count - 1 - mine
    so_far = jax.tree.map(
        lambda part, zero: jnp.full_like(part, 0) + jnp.asarray(zero, part.dtype), value, neutral
    )

    def hop(position, so_far):
        longer = join(so_far, jax.tree.map(lambda part: part[position], pieces))
        return jax.tree.map(lambda new, old: jnp.where(position < mine, new, old), longer, so_far)

    return lax.fori_loop(0, count - 1, hop, so_far)


def decay_tables(log_decay):
    cumulative = jnp.cumsum(log_decay, axis=-1)
    last_cum = cumulative[..., -1:]
    block_len = log_decay.shape[-1]
    row_ids = lax.broadcasted_iota(jnp.int32, (block_len, block_len), 0)
    col_ids = lax.broadcasted_iota(jnp.int32, (block_len, block_len), 1)
    lower_tri = row_ids >= col_ids
    spread = cumulative[..., :, None] - cumulative[..., None, :]
    decay_mask = jnp.where(lower_tri, jnp.exp(jnp.where(lower_tri, spread, 0.0)), 0.0)
    return (cumulative, last_cum, decay_mask)


def to_rows(table):
    return jnp.swapaxes(table, 1, 2)[..., None]


def combine(earlier, latter):
    return (earlier[0] * latter[0], latter[0][..., None, None] * earlier[1] + latter[1])


def local(query_heads, key_heads, value_heads, grad_out, log_decay):
    batch_count, positions, width_all = query_heads.shape
    head_count = log_decay.shape[1]
    head_shape = (batch_count, positions, head_count, width_all // head_count)
    q_split = query_heads.reshape(head_shape)
    k_split = key_heads.reshape(head_shape)
    v_split = value_heads.reshape(head_shape)
    incoming = lax.all_to_all(grad_out, "uly", split_axis=2, concat_axis=1, tiled=True)
    g_split = incoming.reshape(head_shape)
    cumulative, last_cum, decay_mask = decay_tables(log_decay)
    block_keep = jnp.exp(last_cum[..., 0])
    rise_rows = to_rows(jnp.exp(cumulative))
    fall_rows = to_rows(jnp.exp(last_cum - cumulative))
    scaled_query = (rise_rows * q_split).astype(jnp.bfloat16)
    scaled_key = (fall_rows * k_split).astype(jnp.bfloat16)
    update = jnp.einsum("bjhd,bjhe->bhde", scaled_key, v_split, preferred_element_type=jnp.float32)
    local_grad = jnp.einsum(
        "bihd,bihe->bhde", scaled_query, g_split, preferred_element_type=jnp.float32
    )
    state_in = entering(
        (block_keep, update),
        "ctx",
        combine,
        (jnp.ones_like(block_keep), jnp.zeros_like(update)),
        False,
    )[1]
    carried = entering(
        (block_keep, local_grad),
        "ctx",
        combine,
        (jnp.ones_like(block_keep), jnp.zeros_like(local_grad)),
        True,
    )[1]
    scores = jnp.einsum("bihd,bjhd->bhij", q_split, k_split, preferred_element_type=jnp.float32)
    attn_weights = (scores * decay_mask).astype(jnp.bfloat16)
    grad_raw = jnp.einsum("bihe,bjhe->bhij", g_split, v_split, preferred_element_type=jnp.float32)
    grad_scores = (grad_raw * decay_mask).astype(jnp.bfloat16)
    state_b = state_in.astype(jnp.bfloat16)
    attended = jnp.einsum(
        "bhij,bjhd->bihd", attn_weights, v_split, preferred_element_type=jnp.float32
    )
    attended = attended + jnp.einsum(
        "bihd,bhde->bihe", scaled_query, state_b, preferred_element_type=jnp.float32
    )
    query_part = jnp.einsum(
        "bhij,bjhd->bihd", grad_scores, k_split, preferred_element_type=jnp.float32
    )
    query_part = query_part + rise_rows * jnp.einsum(
        "bihe,bhde->bihd", g_split, state_b, preferred_element_type=jnp.float32
    )
    carried_b = carried.astype(jnp.bfloat16)
    key_part = jnp.einsum(
        "bhij,bihd->bjhd", grad_scores, q_split, preferred_element_type=jnp.float32
    )
    key_part = key_part + fall_rows * jnp.einsum(
        "bjhe,bhde->bjhd", v_split, carried_b, preferred_element_type=jnp.float32
    )
    value_part = jnp.einsum(
        "bhij,bihe->bjhe", attn_weights, g_split, preferred_element_type=jnp.float32
    )
    value_part = value_part + fall_rows * jnp.einsum(
        "bjhd,bhde->bjhe", k_split, carried_b, preferred_element_type=jnp.float32
    )

    def to_tokens(array):
        return array.astype(jnp.bfloat16).reshape(batch_count, positions, width_all)

    attended_rows, query_rows, key_rows, value_rows = (
        lax.all_to_all(to_tokens(attended), "uly", split_axis=1, concat_axis=2, tiled=True),
        lax.all_to_all(to_tokens(query_part), "uly", split_axis=1, concat_axis=2, tiled=True),
        lax.all_to_all(to_tokens(key_part), "uly", split_axis=1, concat_axis=2, tiled=True),
        lax.all_to_all(to_tokens(value_part), "uly", split_axis=1, concat_axis=2, tiled=True),
    )
    return (attended_rows, query_rows, key_rows, value_rows)


def solution(mesh):
    placed = (
        P(None, "ctx", "uly"),
        P(None, "ctx", "uly"),
        P(None, "ctx", "uly"),
        P(None, ("ctx", "uly"), None),
        P(None, "uly", "ctx"),
    )
    return jax.shard_map(
        local,
        mesh=mesh,
        in_specs=placed,
        out_specs=(
            P(None, ("ctx", "uly"), None),
            P(None, ("ctx", "uly"), None),
            P(None, ("ctx", "uly"), None),
            P(None, ("ctx", "uly"), None),
        ),
        check_vma=False,
    )
```

profile of v0, /device:TPU:8, one launch (start us, length us, event | category | flops | bytes accessed | tf_op | source)
XLA Modules:
  0.0 278.4 jit_solution(11245880832409896783)
XLA Ops:
  7.9 1.2 reduce-window.6
  9.5 1.1 reshape.285
  12.9 8.4 %copy.172 = bf16[1,16,8192]{1,0,2:T(2,128)(2,1)} copy(bf16[1,16,8192]{2,1,0:T(8,128)(2,1)} %param.12) | data formatting | bytes 524288 | tf_op args[3]
  21.9 45.3 %reduce.1 = bf16[8192,16]{1,0:T(8,128)(2,1)S(1)} reduce(bf16[8192,1,16]{2,1,0:T(2,128)(2,1)} %bitcast.171, bf16[]{:T(256)} %broadcast.69), dimensions={1}, to_apply=%bitcast.141.reduce_sub_computation | reduce | bytes 524290
  67.1 2.8 %reshape.300 = bf16[16,2,4096]{2,1,0:T(2,128)(2,1)} reshape(bf16[8192,16]{1,0:T(8,128)(2,1)S(1)} %reduce.1) | data formatting | bytes 524288
  69.9 9.1 %all-to-all-start.1 = ((bf16[16,2,4096]{2,1,0:T(2,128)(2,1)}), bf16[16,2,4096]{2,1,0:T(2,128)(2,1)S(1)}, u32[]{:S(2)}, u32[]{:S(2)}) async-start(bf16[16,2,4096]{2,1,0:T(2,128)(2,1)} %reshape.300), calls=%async_computation.1 | async-start | bytes 524288 | tf_op jit(solution)/shard_map/all_to_all | solution.py:51
  79.3 6.8 %all-to-all-done.1 = bf16[16,2,4096]{2,1,0:T(2,128)(2,1)S(1)} async-done(((bf16[16,2,4096]{2,1,0:T(2,128)(2,1)}), bf16[16,2,4096]{2,1,0:T(2,128)(2,1)S(1)}, u32[]{:S(2)}, u32[]{:S(2)}) %all-to-all-start.1) | async-done | bytes 262176 | tf_op jit(solution)/shard_map/all_to_all | solution.py:51
  86.1 7.7 %reshape.301 = bf16[8192,1,16]{2,1,0:T(2,128)(2,1)} reshape(bf16[16,2,4096]{2,1,0:T(2,128)(2,1)S(1)} %all-to-all-done.1) | data formatting | bytes 524288
  93.8 7.9 %copy.173 = bf16[1,16,8192]{2,1,0:T(8,128)(2,1)S(1)} copy(bf16[1,16,8192]{1,0,2:T(2,128)(2,1)} %bitcast.172) | data formatting | bytes 524288 | tf_op jit(solution)/shard_map/all_to_all | solution.py:51
  103.2 34.5 %all-gather = f32[32,4,1]{1,2,0:T(1,128)S(1)} all-gather(f32[1,4,1]{1,2,0:T(1,128)S(1)} %get-tuple-element.303), channel_id=2, replica_groups=mesh['ctx'=32,'uly'=16] {'ctx'}, dimensions={0}, use_global_device_ids=true | all-gather | bytes 528 | tf_op jit(solution)/shard_map/all_gather | solution.py:9
  139.7 1.1 convolution_bitcast_fusion.5
  141.1 34.0 %while.28 = (s32[]{:T(128)}, f32[1,4,128,128]{3,2,1,0:T(8,128)S(1)}, s32[]{:T(128)}, f32[32,1,4]{2,1,0:T(1,128)S(1)}, f32[32,1,4,128,128]{4,3,2,1,0:T(8,128)}, /*index=5*/s32[]{:T(128)}, s32[]{:T(128)}) while((s32[]{:T(128)}, f32[1,4,128,128]{3,2,1,0:T(8,128)S(1)}, s32[]{:T(128)}, f32[32,1,4]{2,1,0:T(1,128)S(1)}, ...), condition=%wide.region_3.4_spmd.clone, body=%wide.region_2.3_spmd.clone.sunk | while | flops 262148 | bytes 786585 | solution.py:21
  142.2 1.1 fusion.44
  143.3 1.1 fusion.44
  148.8 1.1 fusion.44
  151.0 1.1 fusion.44
  152.1 1.1 fusion.44
  154.3 1.1 fusion.44
  155.4 1.1 fusion.44
  156.4 1.1 fusion.44
  157.5 1.1 fusion.44
  158.6 1.1 fusion.44
  159.7 1.1 fusion.44
  160.8 1.1 fusion.44
  165.2 1.1 fusion.44
  168.5 1.1 fusion.44
  170.7 1.1 fusion.44
  172.9 1.1 fusion.44
  174.0 1.1 fusion.44
  175.1 1.3 fusion.12
  176.3 1.1 copy.180
  177.5 3.2 %reduce.2 = bf16[256,512]{1,0:T(8,128)(2,1)S(1)} reduce(bf16[256,1,512]{2,1,0:T(2,128)(2,1)} %bitcast.183, bf16[]{:T(256)} %broadcast.69), dimensions={1}, to_apply=%bitcast.143.reduce_sub_computation | reduce | bytes 524290
  181.5 5.1 %all-to-all-start.2 = ((bf16[16,2,4096]{2,1,0:T(2,128)(2,1)}), bf16[16,2,4096]{2,1,0:T(2,128)(2,1)S(1)}, u32[]{:S(2)}, u32[]{:S(2)}) async-start(bf16[16,2,4096]{2,1,0:T(2,128)(2,1)} %reshape.302), calls=%async_computation.2 | async-start | bytes 524288 | tf_op jit(solution)/shard_map/all_to_all | solution.py:113
  187.3 2.3 reduce
  190.5 7.7 %rev.7 = f32[32,1,4,128,128]{4,3,2,1,0:T(8,128)} reverse(f32[32,1,4,128,128]{4,3,2,1,0:T(8,128)} %bitcast.173), dimensions={0} | reverse | bytes 16777216 | tf_op jit(solution)/shard_map/rev | solution.py:11
  198.2 33.8 %while.29 = (s32[]{:T(128)}, f32[1,4,128,128]{3,2,1,0:T(8,128)S(1)}, s32[]{:T(128)}, f32[32,1,4]{2,1,0:T(1,128)S(1)}, f32[32,1,4,128,128]{4,3,2,1,0:T(8,128)}, /*index=5*/s32[]{:T(128)}, s32[]{:T(128)}) while((s32[]{:T(128)}, f32[1,4,128,128]{3,2,1,0:T(8,128)S(1)}, s32[]{:T(128)}, f32[32,1,4]{2,1,0:T(1,128)S(1)}, ...), condition=%wide.region_5.6_spmd.clone, body=%wide.region_4.5_spmd.clone.sunk | while | flops 262148 | bytes 786585 | solution.py:21
  199.3 1.1 fusion.45
  200.4 1.1 fusion.45
  201.5 1.1 fusion.45
  202.6 1.1 fusion.45
  232.0 7.2 %all-to-all-start = ((bf16[16,2,4096]{2,1,0:T(2,128)(2,1)}), bf16[16,2,4096]{2,1,0:T(2,128)(2,1)S(1)}, u32[]{:S(2)}, u32[]{:S(2)}) async-start(bf16[16,2,4096]{2,1,0:T(2,128)(2,1)} %reshape.298), calls=%async_computation | async-start | bytes 524288 | tf_op jit(solution)/shard_map/all_to_all | solution.py:112
  240.0 2.3 reduce.3
  243.1 3.2 %all-to-all-done = bf16[16,2,4096]{2,1,0:T(2,128)(2,1)S(1)} async-done(((bf16[16,2,4096]{2,1,0:T(2,128)(2,1)}), bf16[16,2,4096]{2,1,0:T(2,128)(2,1)S(1)}, u32[]{:S(2)}, u32[]{:S(2)}) %all-to-all-start) | async-done | bytes 262176 | tf_op jit(solution)/shard_map/all_to_all | solution.py:112
  246.3 5.1 %all-to-all-start.3 = ((bf16[16,2,4096]{2,1,0:T(2,128)(2,1)}), bf16[16,2,4096]{2,1,0:T(2,128)(2,1)S(1)}, u32[]{:S(2)}, u32[]{:S(2)}) async-start(bf16[16,2,4096]{2,1,0:T(2,128)(2,1)} %reshape.304), calls=%async_computation.3 | async-start | bytes 524288 | tf_op jit(solution)/shard_map/all_to_all | solution.py:114
  252.2 2.3 reduce.4
  255.3 3.1 %all-to-all-done.3 = bf16[16,2,4096]{2,1,0:T(2,128)(2,1)S(1)} async-done(((bf16[16,2,4096]{2,1,0:T(2,128)(2,1)}), bf16[16,2,4096]{2,1,0:T(2,128)(2,1)S(1)}, u32[]{:S(2)}, u32[]{:S(2)}) %all-to-all-start.3) | async-done | bytes 262176 | tf_op jit(solution)/shard_map/all_to_all | solution.py:114
  258.4 5.2 %all-to-all-start.4 = ((bf16[16,2,4096]{2,1,0:T(2,128)(2,1)}), bf16[16,2,4096]{2,1,0:T(2,128)(2,1)S(1)}, u32[]{:S(2)}, u32[]{:S(2)}) async-start(bf16[16,2,4096]{2,1,0:T(2,128)(2,1)} %reshape.306), calls=%async_computation.4 | async-start | bytes 524288 | tf_op jit(solution)/shard_map/all_to_all | solution.py:115
  266.7 3.9 %all-to-all-done.4 = bf16[16,2,4096]{2,1,0:T(2,128)(2,1)S(1)} async-done(((bf16[16,2,4096]{2,1,0:T(2,128)(2,1)}), bf16[16,2,4096]{2,1,0:T(2,128)(2,1)S(1)}, u32[]{:S(2)}, u32[]{:S(2)}) %all-to-all-start.4) | async-done | bytes 262176 | tf_op jit(solution)/shard_map/all_to_all | solution.py:115
  (171 shorter events, 61.2 us)
Async XLA Ops:
  7.2 133.9 %all-gather.6.cloned.1.call-start = ((), (), s32[]{:S(2)}) async-start(), calls=%async_computation.5 | async-start | bytes 8650752 | tf_op jit(solution)/shard_map/all_gather | solution.py:9
  9.5 69.7 %copy-start = (bf16[1,256,512]{2,1,0:T(8,128)(2,1)S(1)}, bf16[1,256,512]{2,1,0:T(8,128)(2,1)}, u32[]{:S(2)}) copy-start(bf16[1,256,512]{2,1,0:T(8,128)(2,1)} %param.9) | copy-start | bytes 786436
  69.9 16.2 %all-to-all-start.1 = ((bf16[16,2,4096]{2,1,0:T(2,128)(2,1)}), bf16[16,2,4096]{2,1,0:T(2,128)(2,1)S(1)}, u32[]{:S(2)}, u32[]{:S(2)}) async-start(bf16[16,2,4096]{2,1,0:T(2,128)(2,1)} %reshape.300), calls=%async_computation.1 | async-start | bytes 524288 | tf_op jit(solution)/shard_map/all_to_all | solution.py:51
  79.1 111.4 %all-gather.8.cloned.1.call-start = ((), (), s32[]{:S(2)}) async-start(), calls=%async_computation.6 | async-start | bytes 8650752 | tf_op jit(solution)/shard_map/all_gather | solution.py:9
  181.5 50.5 %all-to-all-start.2 = ((bf16[16,2,4096]{2,1,0:T(2,128)(2,1)}), bf16[16,2,4096]{2,1,0:T(2,128)(2,1)S(1)}, u32[]{:S(2)}, u32[]{:S(2)}) async-start(bf16[16,2,4096]{2,1,0:T(2,128)(2,1)} %reshape.302), calls=%async_computation.2 | async-start | bytes 524288 | tf_op jit(solution)/shard_map/all_to_all | solution.py:113
  232.0 14.3 %all-to-all-start = ((bf16[16,2,4096]{2,1,0:T(2,128)(2,1)}), bf16[16,2,4096]{2,1,0:T(2,128)(2,1)S(1)}, u32[]{:S(2)}, u32[]{:S(2)}) async-start(bf16[16,2,4096]{2,1,0:T(2,128)(2,1)} %reshape.298), calls=%async_computation | async-start | bytes 524288 | tf_op jit(solution)/shard_map/all_to_all | solution.py:112
  246.3 12.1 %all-to-all-start.3 = ((bf16[16,2,4096]{2,1,0:T(2,128)(2,1)}), bf16[16,2,4096]{2,1,0:T(2,128)(2,1)S(1)}, u32[]{:S(2)}, u32[]{:S(2)}) async-start(bf16[16,2,4096]{2,1,0:T(2,128)(2,1)} %reshape.304), calls=%async_computation.3 | async-start | bytes 524288 | tf_op jit(solution)/shard_map/all_to_all | solution.py:114
  258.4 12.1 %all-to-all-start.4 = ((bf16[16,2,4096]{2,1,0:T(2,128)(2,1)}), bf16[16,2,4096]{2,1,0:T(2,128)(2,1)S(1)}, u32[]{:S(2)}, u32[]{:S(2)}) async-start(bf16[16,2,4096]{2,1,0:T(2,128)(2,1)} %reshape.306), calls=%async_computation.4 | async-start | bytes 524288 | tf_op jit(solution)/shard_map/all_to_all | solution.py:115
Sparse Core Ops, SparseCore 0:
  13.0 83.9 all-gather.5
  103.3 79.5 all-gather.7
where the time goes:
time: 282 us; the launch traced here: 278 us
  other arithmetic  122 us (43%)
  local copies, waits for them, and re-layouts  50.1 us (18%)
  blocking collectives  34.5 us (12%)
  starting transfers between devices  31.8 us (11%)
  waiting for transfers between devices  17 us (6%)
  between operations  14.4 us (5%)
  matrix products  6.72 us (2%)
    select_n x62, other arithmetic, hop(): jnp.where(position < mine, new, old)  65.4 us
    unnamed x7, other arithmetic  55.2 us
    all_gather x1, blocking collectives, entering(): pieces = jax.tree.map(lambda part: lax.all_gather(part, axis), value)  34.5 us
    unnamed x21, local copies, waits for them, and re-layouts  24.5 us
    all_to_all x1, starting transfers between devices, local(): lax.all_to_all(grad_out, 'uly', split_axis=2, concat_axis=1, tiled=True)  9.14 us
    all_to_all x3, local copies, waits for them, and re-layouts, local(): lax.all_to_all(grad_out, 'uly', split_axis=2, concat_axis=1, tiled=True)  8.03 us
    rev x2, local copies, waits for them, and re-layouts, entering(): pieces = jax.tree.map(lambda part: part[::-1], pieces)  7.8 us
    all_to_all x1, starting transfers between devices, local(): lax.all_to_all(to_tokens(attended), 'uly', split_axis=1, concat_axis=2, t...  7.24 us
  transfers between devices with their start and end apart: 7, of which 4 were waited for; matrix products, arithmetic and copies ran while one was open for 62% of the time, Pallas kernels for 0%

commit v1 on v0

--- a/solution.py
+++ b/solution.py
@@ -2,6 +2,14 @@
 import jax.numpy as jnp
 from jax import lax
 from jax.sharding import PartitionSpec as P
+
+
+def start_clusters_by_axis(tile_in):
+    newest = jax.lax.axis_size("uly")
+    known = jnp.split(tile_in, newest, axis=1)
+    front = jnp.stack(known)
+    inter = jax.lax.all_to_all(front, "uly", split_axis=0, concat_axis=0)
+    return jnp.concatenate(inter, axis=2)
 
 
 def entering(value, axis, join, neutral, backward):
@@ -110,7 +118,7 @@
 
     attended_rows, query_rows, key_rows, value_rows = (
         lax.all_to_all(to_tokens(attended), "uly", split_axis=1, concat_axis=2, tiled=True),
-        lax.all_to_all(to_tokens(query_part), "uly", split_axis=1, concat_axis=2, tiled=True),
+        start_clusters_by_axis(to_tokens(query_part)),
         lax.all_to_all(to_tokens(key_part), "uly", split_axis=1, concat_axis=2, tiled=True),
         lax.all_to_all(to_tokens(value_part), "uly", split_axis=1, concat_axis=2, tiled=True),
     )

time: 282 us -> 337 us (1.20)
  local copies, waits for them, and re-layouts: 50.1 us -> 108 us
  other arithmetic: 122 us -> 118 us
    unnamed x21 -> x53, local copies, waits for them, and re-layouts: 24.5 us -> 60.5 us
    mul x62, local copies, waits for them, and re-layouts: 0.42 us -> 20 us  [combine(): latter[0][..., None, None] * earlier[1] + latter[1]]
    unnamed x7 -> x6, other arithmetic: 55.2 us -> 51.8 us
  transfers between devices with their start and end apart: 7 -> 7, of which waited for: 4 -> 4; matrix products, arithmetic and copies ran while one was open for 62% -> 68% of each run, Pallas kernels for 0% -> 0%
where the time goes in v1:
time: 337 us; the launch traced here: 333 us
  other arithmetic  118 us (35%)
  local copies, waits for them, and re-layouts  108 us (32%)
  blocking collectives  34.5 us (10%)
  starting transfers between devices  31.7 us (9%)
  waiting for transfers between devices  16.4 us (5%)
  between operations  14.4 us (4%)
  matrix products  7.77 us (2%)
    select_n x62, other arithmetic, hop(): jnp.where(position < mine, new, old)  65.3 us
    unnamed x53, local copies, waits for them, and re-layouts  60.5 us
    unnamed x6, other arithmetic  51.8 us
    all_gather x1, blocking collectives, entering(): pieces = jax.tree.map(lambda part: lax.all_gather(part, axis), value)  34.5 us
    mul x62, local copies, waits for them, and re-layouts, combine(): latter[0][..., None, None] * earlier[1] + latter[1]  20 us
    all_to_all x1, starting transfers between devices, local(): lax.all_to_all(grad_out, 'uly', split_axis=2, concat_axis=1, tiled=True)  9.14 us
    all_to_all x3, local copies, waits for them, and re-layouts, local(): lax.all_to_all(grad_out, 'uly', split_axis=2, concat_axis=1, tiled=True)  8.05 us
    rev x2, local copies, waits for them, and re-layouts, entering(): pieces = jax.tree.map(lambda part: part[::-1], pieces)  7.81 us
  transfers between devices with their start and end apart: 7, of which 4 were waited for; matrix products, arithmetic and copies ran while one was open for 68% of the time, Pallas kernels for 0%

profile of v1, /device:TPU:8, one launch (start us, length us, event | category | flops | bytes accessed | tf_op | source)
XLA Modules:
  0.0 332.6 jit_solution(12000075276087398447)
XLA Ops:
  12.9 8.4 %copy.185 = bf16[1,16,8192]{1,0,2:T(2,128)(2,1)} copy(bf16[1,16,8192]{2,1,0:T(8,128)(2,1)} %param.12) | data formatting | bytes 524288 | tf_op args[3]
  21.8 45.2 %reduce.1 = bf16[8192,16]{1,0:T(8,128)(2,1)S(1)} reduce(bf16[8192,1,16]{2,1,0:T(2,128)(2,1)} %bitcast.200, bf16[]{:T(256)} %broadcast.69), dimensions={1}, to_apply=%bitcast.171.reduce_sub_computation | reduce | bytes 524290
  67.0 2.8 reshape.308
  69.8 9.1 %all-to-all-start.1 = ((bf16[16,2,4096]{2,1,0:T(2,128)(2,1)}), bf16[16,2,4096]{2,1,0:T(2,128)(2,1)S(1)}, u32[]{:S(2)}, u32[]{:S(2)}) async-start(bf16[16,2,4096]{2,1,0:T(2,128)(2,1)} %reshape.308), calls=%async_computation.1 | async-start | bytes 524288 | tf_op jit(solution)/shard_map/all_to_all | solution.py:59
  79.3 6.6 %all-to-all-done.1 = bf16[16,2,4096]{2,1,0:T(2,128)(2,1)S(1)} async-done(((bf16[16,2,4096]{2,1,0:T(2,128)(2,1)}), bf16[16,2,4096]{2,1,0:T(2,128)(2,1)S(1)}, u32[]{:S(2)}, u32[]{:S(2)}) %all-to-all-start.1) | async-done | bytes 262176 | tf_op jit(solution)/shard_map/all_to_all | solution.py:59
  86.0 7.6 %reshape.309 = bf16[8192,1,16]{2,1,0:T(2,128)(2,1)} reshape(bf16[16,2,4096]{2,1,0:T(2,128)(2,1)S(1)} %all-to-all-done.1) | data formatting | bytes 524288
  93.6 7.9 %copy.186 = bf16[1,16,8192]{2,1,0:T(8,128)(2,1)S(1)} copy(bf16[1,16,8192]{1,0,2:T(2,128)(2,1)} %bitcast.201) | data formatting | bytes 524288 | tf_op jit(solution)/shard_map/all_to_all | solution.py:59
  103.4 34.5 %all-gather = f32[32,4,1]{1,2,0:T(1,128)S(1)} all-gather(f32[1,4,1]{1,2,0:T(1,128)S(1)} %get-tuple-element.319), channel_id=2, replica_groups=mesh['ctx'=32,'uly'=16] {'ctx'}, dimensions={0}, use_global_device_ids=true | all-gather | bytes 528 | tf_op jit(solution)/shard_map/all_gather | solution.py:17
  141.0 1.3 convolution_bitcast_fusion
  142.3 34.0 %while.28 = (s32[]{:T(128)}, f32[1,4,128,128]{3,2,1,0:T(8,128)S(1)}, s32[]{:T(128)}, f32[32,1,4]{2,1,0:T(1,128)S(1)}, f32[32,1,4,128,128]{4,3,2,1,0:T(8,128)}, /*index=5*/s32[]{:T(128)}, s32[]{:T(128)}) while((s32[]{:T(128)}, f32[1,4,128,128]{3,2,1,0:T(8,128)S(1)}, s32[]{:T(128)}, f32[32,1,4]{2,1,0:T(1,128)S(1)}, ...), condition=%wide.region_3.4_spmd.clone, body=%wide.region_2.3_spmd.clone.sunk | while | flops 262148 | bytes 786585 | solution.py:29
  176.3 1.3 fusion.12
  177.6 1.7 fusion.31
  179.3 1.6 copy.231
  180.8 1.6 copy.232
  182.4 1.6 copy.233
  184.0 1.6 copy.234
  185.6 1.6 copy.235
  187.1 1.6 copy.236
  188.7 1.6 copy.237
  190.3 1.6 copy.238
  191.9 1.6 copy.239
  193.5 1.6 copy.240
  195.0 1.6 copy.241
  197.7 1.3 constant_dynamic-update-slice_fusion.15
  199.0 1.3 constant_dynamic-update-slice_fusion.14
  200.3 1.3 constant_dynamic-update-slice_fusion.13
  201.6 1.3 constant_dynamic-update-slice_fusion.12
  203.0 1.3 constant_dynamic-update-slice_fusion.11
  204.3 1.3 constant_dynamic-update-slice_fusion.10
  205.6 1.3 constant_dynamic-update-slice_fusion.9
  206.9 1.3 constant_dynamic-update-slice_fusion.8
  208.3 1.3 constant_dynamic-update-slice_fusion.7
  209.6 1.3 constant_dynamic-update-slice_fusion.6
  210.9 1.3 constant_dynamic-update-slice_fusion.5
  212.2 1.3 constant_dynamic-update-slice_fusion.4
  216.0 5.1 %all-to-all-start.2 = ((bf16[16,1,16,512]{3,2,1,0:T(8,128)(2,1)}), bf16[16,1,16,512]{3,2,1,0:T(8,128)(2,1)S(1)}, u32[]{:S(2)}, u32[]{:S(2)}) async-start(bf16[16,1,16,512]{3,2,1,0:T(8,128)(2,1)} %constant_dynamic-update-slice_fusion), calls=%async_computation.2 | async-start | bytes 524288 | tf_op jit(solution)/shard_map/all_to_all | solution.py:11
  221.8 2.2 reduce
  224.9 7.7 %rev.7 = f32[32,1,4,128,128]{4,3,2,1,0:T(8,128)} reverse(f32[32,1,4,128,128]{4,3,2,1,0:T(8,128)} %bitcast.202), dimensions={0} | reverse | bytes 16777216 | tf_op jit(solution)/shard_map/rev | solution.py:19
  232.6 52.9 %while.29 = (s32[]{:T(128)}, f32[1,4,128,128]{3,2,1,0:T(8,128)S(1)}, s32[]{:T(128)}, f32[32,1,4]{2,1,0:T(1,128)}, f32[32,1,4,128,128]{4,3,2,1,0:T(8,128)}, /*index=5*/s32[]{:T(128)}, s32[]{:T(128)}) while((s32[]{:T(128)}, f32[1,4,128,128]{3,2,1,0:T(8,128)S(1)}, s32[]{:T(128)}, f32[32,1,4]{2,1,0:T(1,128)}, ...), condition=%wide.region_5.6_spmd.clone, body=%wide.region_4.5_spmd.clone.sunk | while | flops 262148 | bytes 786585 | solution.py:29
  286.2 7.2 %all-to-all-start = ((bf16[16,2,4096]{2,1,0:T(2,128)(2,1)}), bf16[16,2,4096]{2,1,0:T(2,128)(2,1)S(1)}, u32[]{:S(2)}, u32[]{:S(2)}) async-start(bf16[16,2,4096]{2,1,0:T(2,128)(2,1)} %reshape.306), calls=%async_computation | async-start | bytes 524288 | tf_op jit(solution)/shard_map/all_to_all | solution.py:120
  294.1 2.2 reduce.2
  297.2 3.3 all-to-all-done
  300.5 5.1 %all-to-all-start.3 = ((bf16[16,2,4096]{2,1,0:T(2,128)(2,1)}), bf16[16,2,4096]{2,1,0:T(2,128)(2,1)S(1)}, u32[]{:S(2)}, u32[]{:S(2)}) async-start(bf16[16,2,4096]{2,1,0:T(2,128)(2,1)} %reshape.310), calls=%async_computation.3 | async-start | bytes 524288 | tf_op jit(solution)/shard_map/all_to_all | solution.py:122
  306.3 2.2 reduce.3
  309.4 3.2 all-to-all-done.3
  312.6 5.2 %all-to-all-start.4 = ((bf16[16,2,4096]{2,1,0:T(2,128)(2,1)}), bf16[16,2,4096]{2,1,0:T(2,128)(2,1)S(1)}, u32[]{:S(2)}, u32[]{:S(2)}) async-start(bf16[16,2,4096]{2,1,0:T(2,128)(2,1)} %reshape.312), calls=%async_computation.4 | async-start | bytes 524288 | tf_op jit(solution)/shard_map/all_to_all | solution.py:123
  317.7 1.7 copy.249
  321.5 3.2 all-to-all-done.4
  (203 shorter events, 108.9 us)
Async XLA Ops:
  7.2 135.1 %all-gather.6.cloned.1.call-start = ((), (), s32[]{:S(2)}) async-start(), calls=%async_computation.5 | async-start | bytes 8650752 | tf_op jit(solution)/shard_map/all_gather | solution.py:17
  9.6 69.5 %copy-start.2 = (bf16[1,256,512]{2,1,0:T(8,128)(2,1)S(1)}, bf16[1,256,512]{2,1,0:T(8,128)(2,1)}, u32[]{:S(2)}) copy-start(bf16[1,256,512]{2,1,0:T(8,128)(2,1)} %param.9) | copy-start | bytes 786436
  69.8 16.2 %all-to-all-start.1 = ((bf16[16,2,4096]{2,1,0:T(2,128)(2,1)}), bf16[16,2,4096]{2,1,0:T(2,128)(2,1)S(1)}, u32[]{:S(2)}, u32[]{:S(2)}) async-start(bf16[16,2,4096]{2,1,0:T(2,128)(2,1)} %reshape.308), calls=%async_computation.1 | async-start | bytes 524288 | tf_op jit(solution)/shard_map/all_to_all | solution.py:59
  78.9 145.9 %all-gather.8.cloned.1.call-start = ((), (), s32[]{:S(2)}) async-start(), calls=%async_computation.6 | async-start | bytes 8650752 | tf_op jit(solution)/shard_map/all_gather | solution.py:17
  103.4 37.4 %copy-start = (bf16[4,256,256]{2,1,0:T(8,128)(2,1)}, bf16[4,256,256]{2,1,0:T(8,128)(2,1)S(1)}, u32[]{:S(2)}) copy-start(bf16[4,256,256]{2,1,0:T(8,128)(2,1)S(1)} %fusion.2) | copy-start | bytes 1572868
  216.0 69.5 %all-to-all-start.2 = ((bf16[16,1,16,512]{3,2,1,0:T(8,128)(2,1)}), bf16[16,1,16,512]{3,2,1,0:T(8,128)(2,1)S(1)}, u32[]{:S(2)}, u32[]{:S(2)}) async-start(bf16[16,1,16,512]{3,2,1,0:T(8,128)(2,1)} %constant_dynamic-update-slice_fusion), calls=%async_computation.2 | async-start | bytes 524288 | tf_op jit(solution)/shard_map/all_to_all | solution.py:11
  285.5 0.7 copy-start.1
  286.2 14.3 %all-to-all-start = ((bf16[16,2,4096]{2,1,0:T(2,128)(2,1)}), bf16[16,2,4096]{2,1,0:T(2,128)(2,1)S(1)}, u32[]{:S(2)}, u32[]{:S(2)}) async-start(bf16[16,2,4096]{2,1,0:T(2,128)(2,1)} %reshape.306), calls=%async_computation | async-start | bytes 524288 | tf_op jit(solution)/shard_map/all_to_all | solution.py:120
  300.5 12.0 %all-to-all-start.3 = ((bf16[16,2,4096]{2,1,0:T(2,128)(2,1)}), bf16[16,2,4096]{2,1,0:T(2,128)(2,1)S(1)}, u32[]{:S(2)}, u32[]{:S(2)}) async-start(bf16[16,2,4096]{2,1,0:T(2,128)(2,1)} %reshape.310), calls=%async_computation.3 | async-start | bytes 524288 | tf_op jit(solution)/shard_map/all_to_all | solution.py:122
  312.6 12.1 %all-to-all-start.4 = ((bf16[16,2,4096]{2,1,0:T(2,128)(2,1)}), bf16[16,2,4096]{2,1,0:T(2,128)(2,1)S(1)}, u32[]{:S(2)}, u32[]{:S(2)}) async-start(bf16[16,2,4096]{2,1,0:T(2,128)(2,1)} %reshape.312), calls=%async_computation.4 | async-start | bytes 524288 | tf_op jit(solution)/shard_map/all_to_all | solution.py:123
Sparse Core Ops, SparseCore 0:
  13.0 83.9 all-gather.5
  103.1 79.9 all-gather.7
